TPU v7x, 512 devices: a whole 4x4x16 slice. The times are simulated.
512 devices in a mesh: dp: 8 (over z_lo), seq: 4 (over z_hi, core), expert: 16 (over x, y).
Axes of the slice: x: 4, y: 4, z: 16 (z_hi: 2, z_lo: 8; z = z_hi * 8 + z_lo), core: 2. Of those that a mesh axis runs over, the one named last changes fastest.
Arguments:
- keys: bfloat16 [16, 4096, 512], P('expert', ('dp', 'seq')), may hold values from -4 to 4
- values: bfloat16 [16, 4096, 512], P('expert', ('dp', 'seq')), may hold values from -5 to 5
- queries: bfloat16 [16, 32, 4096], P('expert', ('dp', 'seq')), may hold values from -80 to 80
- residual: bfloat16 [16, 32, 2048], P('expert', ('dp', 'seq')), may hold values from -9 to 9
- out_proj: bfloat16 [4096, 2048], P(('dp', 'seq')), may hold values from -0.09375 to 0.09375
- norm_gain: bfloat16 [2048], replicated, may hold values from 0.25 to 1.75
- router: bfloat16 [2048, 128], replicated, may hold values from -8 to 8
- w_gate: bfloat16 [128, 2048, 768], P(('dp', 'expert'), None, 'seq'), may hold values from -0.125 to 0.125
- w_up: bfloat16 [128, 2048, 768], P(('dp', 'expert'), None, 'seq'), may hold values from -0.125 to 0.125
- w_down: bfloat16 [128, 768, 2048], P(('dp', 'expert'), 'seq'), may hold values from -0.21875 to 0.21875
- head_vec: bfloat16 [2048], replicated, may hold values from -0.09 to 0.09
- routes: int32 [16, 32, 8], P('expert', 'dp'), may hold values from 0 to 127, all different within a row; in each aligned block of 4 rows (0 to 3, 4 to 7, ..., all dimensions but the last counted through in order) at most 2 rows name the same one
- step_pos: int32 [16, 32], P('expert'), may hold values from 0 to 4095, as said below
- labels: int32 [16, 32], P('expert', ('dp', 'seq')), may hold values 0 or 1
- trace_len: int32 [16, 8], P('expert'), may hold values from 1 to 1024, 4096 in all within a row
Outputs:
- loss: float32 [], replicated
- grad_down: bfloat16 [128, 768, 2048], P(('dp', 'expert'), 'seq')
- grad_router: bfloat16 [2048, 128], P(('dp', 'seq', 'expert'))
Inputs may be any that keep to these rules, and one draw needn't show every extreme that they name: `step_pos`: increasing along each pack; distinct. `routes`: in each aligned block of 4 step ends (those of one index of dp in one pack) no expert is named by more than 2 of them.
All inputs are finite; a program needn't handle non-finite values. No bound on the sum of `labels` on one device may be relied on, other than what follows from the above.
Results may differ from a plain program's by a relative error of at most 0.018.
Values may be sent and summed in bfloat16 or wider, within the bound.
No kernel may reach another device: no remote copies, remote signals or barrier semaphores. Data moves between devices by JAX's collectives and lax.ppermute only.
A program may use at most 64 MiB of HBM per device.

v0:
```python
import jax
import jax.numpy as jnp
from jax import lax
from jax.sharding import Mesh
from jax.sharding import PartitionSpec as P

QUERY_HEADS = 32
KEY_VALUE_HEADS = 4
HEAD_WIDTH = 128
DP_EXPERT = ("dp", "expert_0", "expert_1")
DP_SEQ = ("dp", "seq_0", "seq_1")
SEQ = ("seq_0", "seq_1")
DP_SEQ_EXPERT = ("dp", "seq_0", "seq_1", "expert_0", "expert_1")
EXPERT = ("expert_0", "expert_1")
ROWS = DP_SEQ_EXPERT
MASKED = -1e30
EPSILON = 1e-06


def joined_along(blocks, dim):
    blocks = jnp.moveaxis(blocks, 0, dim)
    lengths = blocks.shape
    return blocks.reshape(*lengths[:dim], lengths[dim] * lengths[dim + 1], *lengths[dim + 2 :])


def from_everyone(array, axis):
    copies = jnp.broadcast_to(array, (lax.axis_size(axis), *array.shape))
    return lax.all_to_all(copies, axis, split_axis=0, concat_axis=0, tiled=True)


def gather_directly(array, axis, dim):
    return joined_along(from_everyone(array, axis), dim)


def in_blocks(array, dim, count):
    lengths = array.shape
    blocks = array.reshape(*lengths[:dim], count, lengths[dim] // count, *lengths[dim + 1 :])
    return jnp.moveaxis(blocks, dim, 0)


def sent_and_summed(array, axis, dim):
    count = lax.axis_size(axis)
    blocks = lax.all_to_all(in_blocks(array, dim, count), axis, 0, 0, tiled=True)
    return jnp.sum(blocks.astype(jnp.float32), axis=0)


def rms_scale(stream):
    return lax.rsqrt(jnp.mean(stream * stream, axis=-1, keepdims=True) + EPSILON)


def head_logit(final, head_vec):
    return jnp.sum(final * rms_scale(final) * head_vec.astype(jnp.float32)[None, :], axis=1)


def split_pair(value):
    high = value.astype(jnp.bfloat16)
    low = (value - high.astype(jnp.float32)).astype(jnp.bfloat16)
    return (high, low)


def join_pair(high, low):
    return high.astype(jnp.float32) + low.astype(jnp.float32)


def merge_heads(weighted_r, totals_r, peak_r):
    peak_all = jnp.max(peak_r, axis=0)
    factor = jnp.exp(peak_r - peak_all[None])
    weighted_sum = jnp.sum(weighted_r * factor[..., None], axis=0)
    totals_sum = jnp.sum(totals_r * factor, axis=0)
    merged = weighted_sum / totals_sum[..., None]
    return merged.reshape(merged.shape[0], -1).astype(jnp.bfloat16)


def shards(
    keys,
    values,
    queries,
    residual,
    out_proj,
    norm_gain,
    router,
    w_gate,
    w_up,
    w_down,
    head_vec,
    routes,
    step_pos,
    labels,
    trace_len,
):
    block_routes = lax.all_gather(routes[0], DP_EXPERT, axis=0)
    block_routes = block_routes.reshape(
        lax.axis_size("dp"), lax.axis_size(EXPERT), *routes.shape[1:]
    )
    routes_all = jnp.swapaxes(block_routes, 1, 2).reshape(-1, routes.shape[2])
    count_of_keys = keys.shape[1]
    query_groups = QUERY_HEADS // KEY_VALUE_HEADS
    query_all = gather_directly(queries, DP_SEQ, 1)[0]
    positions = step_pos[0]
    number_of_steps = positions.shape[0]
    lengths = trace_len[0]
    trace_ends = jnp.cumsum(lengths)
    starts = jnp.sum(
        jnp.where(trace_ends[None, :] <= positions[:, None], lengths[None, :], 0), axis=1
    )
    key_pos = lax.axis_index(DP_SEQ) * count_of_keys + jnp.arange(count_of_keys, dtype=jnp.int32)
    allowed = (key_pos[None, :] <= positions[:, None]) & (key_pos[None, :] >= starts[:, None])
    score_list = []
    for head_cluster in range(KEY_VALUE_HEADS):
        query_part = query_all[
            :,
            head_cluster
            * query_groups
            * HEAD_WIDTH : (head_cluster + 1)
            * query_groups
            * HEAD_WIDTH,
        ].reshape(number_of_steps * query_groups, HEAD_WIDTH)
        key_part = keys[0, :, head_cluster * HEAD_WIDTH : (head_cluster + 1) * HEAD_WIDTH]
        score_part = lax.dot_general(
            query_part, key_part, (((1,), (1,)), ((), ())), preferred_element_type=jnp.float32
        ) * HEAD_WIDTH ** (-0.5)
        score_part = score_part.reshape(number_of_steps, query_groups, count_of_keys)
        score_list.append(jnp.where(allowed[:, None, :], score_part, MASKED))
    scores = jnp.stack(score_list, axis=1).reshape(number_of_steps, QUERY_HEADS, count_of_keys)
    local_peak = jnp.max(scores, axis=2)
    heads_of_values = values[0].reshape(count_of_keys, KEY_VALUE_HEADS, HEAD_WIDTH)
    complete_weight_rows = jnp.where(
        allowed[:, None, :], jnp.exp(scores - local_peak[:, :, None]), 0.0
    )
    totals = jnp.sum(complete_weight_rows, axis=2)
    reduced_weight_rows = complete_weight_rows.astype(jnp.bfloat16).reshape(
        number_of_steps, KEY_VALUE_HEADS, query_groups, count_of_keys
    )
    weighted = jnp.einsum(
        "skgt,tkd->skgd", reduced_weight_rows, heads_of_values, preferred_element_type=jnp.float32
    ).reshape(number_of_steps, QUERY_HEADS, HEAD_WIDTH)
    totals_hi, totals_lo = split_pair(totals)
    peak_hi, peak_lo = split_pair(local_peak)
    packed = jnp.concatenate(
        [
            weighted.astype(jnp.bfloat16),
            totals_hi[..., None],
            totals_lo[..., None],
            peak_hi[..., None],
            peak_lo[..., None],
        ],
        axis=-1,
    )
    arrived = lax.all_to_all(
        packed.reshape(1, *packed.shape), DP_SEQ, split_axis=2, concat_axis=0, tiled=True
    )
    attn = merge_heads(
        arrived[..., :HEAD_WIDTH].astype(jnp.float32),
        join_pair(arrived[..., HEAD_WIDTH], arrived[..., HEAD_WIDTH + 1]),
        join_pair(arrived[..., HEAD_WIDTH + 2], arrived[..., HEAD_WIDTH + 3]),
    )
    mixed = sent_and_summed(
        jnp.dot(attn, out_proj, preferred_element_type=jnp.float32).astype(jnp.bfloat16), DP_SEQ, 0
    )
    stream = residual[0].astype(jnp.float32) + mixed
    normed = (stream * rms_scale(stream) * norm_gain.astype(jnp.float32)[None, :]).astype(
        jnp.bfloat16
    )
    normed_all = lax.all_gather(normed, ROWS, axis=0, tiled=True)
    experts = router.shape[1]
    logits = jnp.dot(normed_all, router, preferred_element_type=jnp.float32)
    chosen = (routes_all[:, :, None] == jnp.arange(experts, dtype=jnp.int32)[None, None, :]).astype(
        jnp.float32
    )
    picked = jnp.sum(chosen * logits[:, None, :], axis=2)
    gate_weight = jax.nn.softmax(picked, axis=-1)
    mine = routes_all == lax.axis_index(DP_EXPERT)
    coef = jnp.sum(jnp.where(mine, gate_weight, 0.0), axis=1)
    gate_act = jnp.dot(normed_all, w_gate[0], preferred_element_type=jnp.float32)
    up_act = jnp.dot(normed_all, w_up[0], preferred_element_type=jnp.float32)
    hidden = (jax.nn.silu(gate_act) * up_act).astype(jnp.bfloat16)
    expert_out = jnp.dot(hidden, w_down[0], preferred_element_type=jnp.float32)
    expert_mix = lax.psum_scatter(coef[:, None] * expert_out, ROWS, scatter_dimension=0, tiled=True)
    final = stream + expert_mix
    reward, pull = jax.vjp(lambda value: head_logit(value, head_vec), final)
    target = labels[0].astype(jnp.float32)
    loss_term = jax.nn.softplus(reward) - target * reward
    logit_grad = jax.nn.sigmoid(reward) - target
    (final_grad,) = pull(logit_grad)
    d_mix = final_grad.astype(jnp.bfloat16)
    d_mix_all = lax.all_gather(d_mix, ROWS, axis=0, tiled=True)
    d_mix_wide = d_mix_all.astype(jnp.float32)
    contract_rows = (((0,), (0,)), ((), ()))
    d_out = (coef[:, None] * d_mix_wide).astype(jnp.bfloat16)
    grad_down = lax.dot_general(hidden, d_out, contract_rows, preferred_element_type=jnp.float32)
    grad_down = grad_down.astype(jnp.bfloat16).reshape((1,) + grad_down.shape)
    share_dot = jnp.sum(d_mix_wide * expert_out, axis=1)
    row_count = normed_all.shape[0]
    own_row = jnp.arange(row_count, dtype=jnp.int32) == lax.axis_index(ROWS)
    payload = jnp.concatenate(
        [jnp.where(mine, share_dot[:, None], 0.0), jnp.where(own_row, loss_term, 0.0)[:, None]],
        axis=1,
    )
    summed = lax.psum(payload, ROWS)
    route_dot = summed[:, :-1]
    loss = jnp.sum(summed[:, -1])
    pick_grad = gate_weight * (route_dot - jnp.sum(gate_weight * route_dot, axis=1, keepdims=True))
    d_logits = jnp.sum(chosen * pick_grad[:, :, None], axis=1)
    router_grad_all = lax.dot_general(
        normed_all.astype(jnp.float32), d_logits, contract_rows, precision=lax.Precision.HIGHEST
    )
    own_rows = router_grad_all.shape[0] // lax.axis_size(DP_SEQ_EXPERT)
    grad_router = lax.dynamic_slice_in_dim(
        router_grad_all, lax.axis_index(DP_SEQ_EXPERT) * own_rows, own_rows, axis=0
    ).astype(jnp.bfloat16)
    return (loss, grad_down, grad_router)


def solution(mesh):
    finer = Mesh(
        mesh.devices.reshape(mesh.shape["dp"], 2, 2, 4, 4),
        ("dp", "seq_0", "seq_1", "expert_0", "expert_1"),
    )
    return jax.shard_map(
        shards,
        mesh=finer,
        in_specs=(
            P(EXPERT, DP_SEQ, None),
            P(EXPERT, DP_SEQ, None),
            P(EXPERT, DP_SEQ, None),
            P(EXPERT, DP_SEQ, None),
            P(DP_SEQ, None),
            P(),
            P(),
            P(DP_EXPERT, None, SEQ),
            P(DP_EXPERT, None, SEQ),
            P(DP_EXPERT, SEQ, None),
            P(),
            P(EXPERT, "dp", None),
            P(EXPERT, None),
            P(EXPERT, DP_SEQ),
            P(EXPERT, None),
        ),
        out_specs=(P(), P(DP_EXPERT, SEQ, None), P(DP_SEQ_EXPERT, None)),
        check_vma=False,
    )
```

profile of v0, /device:TPU:1, one launch (start us, length us, event | category | flops | bytes accessed | tf_op | source)
XLA Modules:
  0.0 3206.8 jit_solution(4722802899857417348)
XLA Ops:
  7.2 0.8 reduce.14
  8.1 0.5 broadcast_in_dim.130
  8.5 0.5 broadcast.181
  9.0 2.2 reduce.15
  11.3 0.9 reshape.490
  12.1 16.7 all-to-all-start
  29.3 18.7 all-to-all-done
  52.1 0.6 concatenate.6
  53.0 32.4 %all_to_all.28 = bf16[1,32,32,132]{3,1,0,2:T(8,128)(2,1)S(1)} all-to-all(bf16[1,32,32,132]{3,1,0,2:T(8,128)(2,1)S(1)} %copy.165), channel_id=1, replica_groups=mesh['dp'=8,'seq_0'=2,'seq_1'=2,'expert_0'=4,'expert_1'=4] {'dp','seq_0'..., dimensions={2} | all-to-all | bytes 540672 | tf_op jit(solution)/shard_map/all_to_all | solution.py:149
  85.4 1.1 copy.166
  86.6 0.5 multiply_reduce_fusion
  87.3 0.7 reduce.16
  88.0 0.7 reshape.492
  88.7 9.7 all-to-all-start.2
  98.5 15.2 all-to-all-done.2
  114.0 0.6 copy-done.9
  114.6 0.6 multiply_reduce_fusion.5
  115.9 0.6 multiply_convert_fusion
  116.6 462.9 %all_gather.9 = s32[128,4,8]{2,1,0:T(4,128)S(1)} all-gather(s32[1,4,8]{2,1,0:T(4,128)S(1)} %copy-done.17), channel_id=1, replica_groups=mesh['dp'=8,'seq_0'=2,'seq_1'=2,'expert_0'=4,'expert_1'=4] {'dp','expert..., dimensions={0}, use_global_device_ids=true | all-gather | bytes 16512 | tf_op jit(solution)/shard_map/all_gather | solution.py:91
  580.5 593.1 %all-gather.5.cloned.1.call-done = bf16[1048576]{0:T(1024)(128)(2,1)} async-done(((bf16[2048]{0:T(1024)(128)(2,1)}), bf16[1048576]{0:T(1024)(128)(2,1)}) %all-gather.5.cloned.1.call-update) | async-done | bytes 2097168 | tf_op jit(solution)/shard_map/all_gather | solution.py:164
  1173.6 2.8 reshape.484
  1176.4 2.8 fusion.21
  1179.2 0.7 fusion.51
  1179.9 7.3 select_reduce_fusion.1
  1187.3 0.8 reduce_max.32
  1188.1 1.4 sub.91
  1189.4 1.3 fusion.45
  1190.7 1.4 div.48
  1192.1 1.3 copy.173
  1193.4 0.8 copy.171
  1194.2 0.7 copy.170
  1194.9 0.9 select_reduce_fusion.2
  1195.9 2.1 fusion.7
  1198.0 4.1 broadcast_multiply_fusion
  1202.2 0.6 copy-done.15
  1203.5 480.3 %all-reduce.3.cloned.1.call-done = f32[512,2048]{1,0:T(8,128)} async-done(((f32[512,2048]{1,0:T(8,128)}), f32[512,2048]{1,0:T(8,128)}) %all-reduce.3.cloned.1.call-update) | async-done | bytes 4194320
  1683.8 1.5 multiply_reduce_fusion.4
  1686.0 0.6 multiply_reduce_fusion.3
  1687.3 0.6 multiply_reduce_fusion.2
  1688.6 0.6 fusion.47
  1693.2 1384.5 %all-gather.7.cloned.1.call-done = bf16[512,1,2048]{2,1,0:T(2,128)(2,1)} async-done(((bf16[1,1,2048]{2,1,0:T(2,128)(2,1)}), bf16[512,1,2048]{2,1,0:T(2,128)(2,1)}) %all-gather.7.cloned.1.call-update) | async-done | bytes 2097168 | tf_op jit(solution)/shard_map/all_gather | solution.py:186
  3077.8 4.8 fusion
  3082.6 106.9 %psum.7 = f32[512,9]{0,1:T(8,128)S(1)} all-reduce(f32[512,9]{0,1:T(8,128)S(1)} %pad_maximum_fusion.2), channel_id=1, replica_groups=mesh['dp'=8,'seq_0'=2,'seq_1'=2,'expert_0'=4,'expert_1'=4] {'dp','seq_0'..., use_global_device_ids=true, to_apply=%region_18.19 | all-reduce | flops 4608 | bytes 36864 | tf_op jit(solution)/shard_map/psum | solution.py:199
  3189.6 0.6 slice_reduce_fusion
  3190.3 2.5 select_reduce_fusion
  3192.8 2.3 fusion.52
  3195.1 0.6 dynamic-slice_convert_fusion
  3195.7 4.6 fusion.2
  (97 shorter events, 6.9 us)
Async XLA Ops:
  7.2 1190.9 %copy-start = (bf16[1,192,2048]{2,1,0:T(8,128)(2,1)S(1)}, bf16[1,192,2048]{2,1,0:T(8,128)(2,1)}, u32[]{:S(2)}) copy-start(bf16[1,192,2048]{2,1,0:T(8,128)(2,1)} %param.24) | copy-start | bytes 2359300
  7.2 21.7 copy-start.8
  7.2 21.8 copy-start.19
  7.2 22.0 copy-start.18
  9.0 39.7 %copy-start.7 = (bf16[1,128,512]{2,1,0:T(8,128)(2,1)S(1)}, bf16[1,128,512]{2,1,0:T(8,128)(2,1)}, u32[]{:S(2)}) copy-start(bf16[1,128,512]{2,1,0:T(8,128)(2,1)} %param.15) | copy-start | bytes 393220
  12.1 35.9 %all-to-all-start = ((bf16[32,2,2048]{2,1,0:T(2,128)(2,1)}), bf16[32,2,2048]{2,1,0:T(2,128)(2,1)S(1)}, u32[]{:S(2)}, u32[]{:S(2)}) async-start(bf16[32,2,2048]{2,1,0:T(2,128)(2,1)} %reshape.490), calls=%async_computation | async-start | bytes 524288 | tf_op jit(solution)/shard_map/all_to_all | solution.py:28
  53.0 34.1 %copy-start.1 = (bf16[128,2048]{1,0:T(8,128)(2,1)S(1)}, bf16[128,2048]{1,0:T(8,128)(2,1)}, u32[]{:S(2)}) copy-start(bf16[128,2048]{1,0:T(8,128)(2,1)} %param.19) | copy-start | bytes 1572868
  85.3 13.1 copy-start.13
  86.5 29.4 copy-start.16
  86.5 30.1 copy-start.17
  88.7 25.0 all-to-all-start.2
  98.4 1075.2 %all-gather.5.cloned.1.call-start = ((), (), s32[]{:S(2)}) async-start(), calls=%async_computation.3 | async-start | bytes 2101248 | tf_op jit(solution)/shard_map/all_gather | solution.py:164
  114.0 0.6 copy-start.9
  116.5 1567.2 %all-reduce.3.cloned.1.call-start = ((), (), s32[]{:S(2)}) async-start(), calls=%async_computation.5 | async-start | bytes 8388608
  579.9 0.6 copy-start.5
  1176.4 2.8 copy-start.2
  1198.0 4.1 copy-start.3
  1202.1 0.7 copy-start.15
  1202.1 481.7 %copy-start.10 = (f32[2048]{0:T(1024)S(1)}, f32[2048]{0:T(1024)}, u32[]{:S(2)}) copy-start(f32[2048]{0:T(1024)} %copy-done.9) | copy-start | bytes 24580
  1202.1 481.7 %copy-start.14 = (bf16[1,1,2048]{2,1,0:T(2,128)(2,1)S(1)}, bf16[1,1,2048]{2,1,0:T(2,128)(2,1)}, u32[]{:S(2)}) copy-start(bf16[1,1,2048]{2,1,0:T(2,128)(2,1)} %param.18) | copy-start | bytes 12292
  1202.2 1875.6 %all-gather.7.cloned.1.call-start = ((), (), s32[]{:S(2)}) async-start(), calls=%async_computation.4 | async-start | bytes 4202496 | tf_op jit(solution)/shard_map/all_gather | solution.py:186
  3077.8 4.8 copy-start.6
  3077.8 111.8 %copy-start.11 = (f32[512]{0:T(512)S(1)}, f32[512]{0:T(512)}, u32[]{:S(2)}) copy-start(f32[512]{0:T(512)} %reduce_max.32) | copy-start | bytes 6148
  3077.8 111.8 %copy-start.12 = (f32[512]{0:T(512)S(1)}, f32[512]{0:T(512)}, u32[]{:S(2)}) copy-start(f32[512]{0:T(512)} %fusion.45) | copy-start | bytes 6148
  3190.3 5.4 copy-start.4
Sparse Core Ops, SparseCore 0:
  116.7 1056.8 all-gather.4
  1202.3 481.4 all-reduce.2
  1689.4 1388.3 all-gather.6
where the time goes:
time: 3210 us
  waiting for transfers between devices  2490 us (78%)
  blocking collectives  602 us (19%)
    all_gather x1, waiting for transfers between devices, shards(): d_mix_all = lax.all_gather(d_mix, ROWS, axis=0, tiled=True)  1380 us
    all_gather x1, waiting for transfers between devices, shards(): normed_all = lax.all_gather(normed, ROWS, axis=0, tiled=True)  593 us
    unnamed x4, waiting for transfers between devices  480 us
    all_gather x1, blocking collectives, shards(): block_routes = lax.all_gather(routes[0], DP_EXPERT, axis=0)  463 us
    psum x1, blocking collectives, shards(): summed = lax.psum(payload, ROWS)  107 us
  transfers between devices with their start and end apart: 5, of which 5 were waited for; matrix products, arithmetic and copies ran while one was open for 0% of the time, Pallas kernels for 0%

commit v1 on v0

--- a/solution.py
+++ b/solution.py
@@ -196,7 +196,7 @@
         [jnp.where(mine, share_dot[:, None], 0.0), jnp.where(own_row, loss_term, 0.0)[:, None]],
         axis=1,
     )
-    summed = lax.psum(payload, ROWS)
+    summed = jnp.sum(lax.all_gather(payload, ROWS), axis=0)
     route_dot = summed[:, :-1]
     loss = jnp.sum(summed[:, -1])
     pick_grad = gate_weight * (route_dot - jnp.sum(gate_weight * route_dot, axis=1, keepdims=True))

time: 3210 us -> 4550 us (1.42)
  waiting for transfers between devices: 2490 us -> 3920 us
  blocking collectives: 602 us -> 495 us
    all_gather x0 -> x1, waiting for transfers between devices: none -> 1430 us  [shards(): summed = jnp.sum(lax.all_gather(payload, ROWS), axis=0)]
    psum x1 -> x0, blocking collectives: 107 us -> none  [shards(): summed = lax.psum(payload, ROWS)]
    unnamed x4 -> x5, waiting for transfers between devices: 480 us -> 481 us
  transfers between devices with their start and end apart: 5 -> 6, of which waited for: 5 -> 6; matrix products, arithmetic and copies ran while one was open for 0% -> 0% of each run, Pallas kernels for 0% -> 0%
where the time goes in v1:
time: 4550 us
  waiting for transfers between devices  3920 us (86%)
  blocking collectives  495 us (11%)
    all_gather x1, waiting for transfers between devices, shards(): summed = jnp.sum(lax.all_gather(payload, ROWS), axis=0)  1430 us
    all_gather x1, waiting for transfers between devices, shards(): d_mix_all = lax.all_gather(d_mix, ROWS, axis=0, tiled=True)  1380 us
    all_gather x1, waiting for transfers between devices, shards(): normed_all = lax.all_gather(normed, ROWS, axis=0, tiled=True)  593 us
    unnamed x5, waiting for transfers between devices  481 us
    all_gather x1, blocking collectives, shards(): block_routes = lax.all_gather(routes[0], DP_EXPERT, axis=0)  463 us
  transfers between devices with their start and end apart: 6, of which 6 were waited for; matrix products, arithmetic and copies ran while one was open for 0% of the time, Pallas kernels for 0%

profile of v1, /device:TPU:1, one launch (start us, length us, event | category | flops | bytes accessed | tf_op | source)
XLA Modules:
  0.0 4548.4 jit_solution(8149939716975878739)
XLA Ops:
  7.2 0.8 reduce.14
  8.5 0.5 broadcast.181
  9.0 2.2 reduce.15
  11.3 0.9 reshape.491
  12.1 16.7 all-to-all-start
  29.3 18.7 all-to-all-done
  52.1 0.5 concatenate.6
  52.9 32.4 all_to_all.28
  85.3 1.1 copy.167
  87.3 0.7 reduce.16
  88.0 0.7 reshape.493
  88.7 9.7 all-to-all-start.2
  98.5 15.2 all-to-all-done.2
  114.0 0.6 copy-done.7
  114.6 0.6 multiply_reduce_fusion.5
  115.9 0.6 multiply_convert_fusion
  116.6 462.9 %all_gather.15 = s32[128,4,8]{2,1,0:T(4,128)S(1)} all-gather(s32[1,4,8]{2,1,0:T(4,128)S(1)} %copy-done.15), channel_id=1, replica_groups=mesh['dp'=8,'seq_0'=2,'seq_1'=2,'expert_0'=4,'expert_1'=4] {'dp','expert..., dimensions={0}, use_global_device_ids=true | all-gather | bytes 16512 | tf_op jit(solution)/shard_map/all_gather | solution.py:91
  580.4 593.1 %all-gather.7.cloned.1.call-done = bf16[1048576]{0:T(1024)(128)(2,1)} async-done(((bf16[2048]{0:T(1024)(128)(2,1)}), bf16[1048576]{0:T(1024)(128)(2,1)}) %all-gather.7.cloned.1.call-update) | async-done | bytes 2097168 | tf_op jit(solution)/shard_map/all_gather | solution.py:164
  1173.5 2.8 reshape.484
  1176.4 1.8 fusion.51
  1178.1 7.3 select_reduce_fusion.1
  1185.5 0.8 reduce_max.32
  1186.3 1.4 sub.91
  1187.6 1.3 fusion.45
  1188.9 1.4 div.48
  1190.3 1.3 copy.174
  1191.6 1.3 copy.171
  1192.9 0.8 copy.172
  1193.7 1.0 select_reduce_fusion.2
  1194.8 2.0 fusion.21
  1196.9 0.9 fusion.7
  1197.7 4.1 broadcast_multiply_fusion
  1202.6 480.6 %all-reduce.3.cloned.1.call-done = f32[512,2048]{1,0:T(8,128)} async-done(((f32[512,2048]{1,0:T(8,128)}), f32[512,2048]{1,0:T(8,128)}) %all-reduce.3.cloned.1.call-update) | async-done | bytes 4194320
  1683.2 1.5 multiply_reduce_fusion.4
  1685.4 0.6 multiply_reduce_fusion.3
  1686.7 0.6 multiply_reduce_fusion.2
  1688.0 0.6 fusion.47
  1692.9 1384.3 %all-gather.11.cloned.1.call-done = bf16[512,1,2048]{2,1,0:T(2,128)(2,1)} async-done(((bf16[1,1,2048]{2,1,0:T(2,128)(2,1)}), bf16[512,1,2048]{2,1,0:T(2,128)(2,1)}) %all-gather.11.cloned.1.call-update) | async-done | bytes 2097168 | tf_op jit(solution)/shard_map/all_gather | solution.py:186
  3077.2 4.8 fusion
  3082.0 0.6 pad_maximum_fusion.2
  3082.6 4.6 fusion.2
  3087.2 1432.3 %all-gather.9.cloned.1.call-done = f32[262144,9]{0,1:T(8,128)} async-done(((f32[512,9]{0,1:T(8,128)}), f32[262144,9]{0,1:T(8,128)}) %all-gather.9.cloned.1.call-update) | async-done | bytes 9437200 | tf_op jit(solution)/shard_map/all_gather | solution.py:199
  4519.5 15.2 copy.185
  4534.7 0.9 bitcast_reduce_fusion
  4535.6 0.6 slice_reduce_fusion
  4536.4 2.5 select_reduce_fusion
  4538.9 2.3 fusion.52
  4541.2 0.6 dynamic-slice_convert_fusion
  (99 shorter events, 8.1 us)
Async XLA Ops:
  7.2 1190.6 %copy-start = (bf16[1,192,2048]{2,1,0:T(8,128)(2,1)S(1)}, bf16[1,192,2048]{2,1,0:T(8,128)(2,1)}, u32[]{:S(2)}) copy-start(bf16[1,192,2048]{2,1,0:T(8,128)(2,1)} %param.24) | copy-start | bytes 2359300
  7.2 21.7 copy-start.6
  7.2 21.8 copy-start.17
  7.2 22.0 copy-start.16
  9.0 39.7 copy-start.5
  12.1 35.9 all-to-all-start
  52.9 34.1 copy-start.2
  85.3 13.1 copy-start.11
  86.4 29.4 copy-start.14
  86.5 30.1 copy-start.15
  88.7 25.0 all-to-all-start.2
  98.4 1075.2 %all-gather.7.cloned.1.call-start = ((), (), s32[]{:S(2)}) async-start(), calls=%async_computation.3 | async-start | bytes 2101248 | tf_op jit(solution)/shard_map/all_gather | solution.py:164
  114.0 0.6 copy-start.7
  116.5 1566.6 %all-reduce.3.cloned.1.call-start = ((), (), s32[]{:S(2)}) async-start(), calls=%async_computation.6 | async-start | bytes 8388608
  579.8 0.6 copy-start.3
  1194.8 2.1 copy-start.18
  1201.8 0.7 copy-start.13
  1201.8 481.4 %copy-start.8 = (f32[2048]{0:T(1024)S(1)}, f32[2048]{0:T(1024)}, u32[]{:S(2)}) copy-start(f32[2048]{0:T(1024)} %copy-done.7) | copy-start | bytes 24580
  1201.8 481.4 %copy-start.12 = (bf16[1,1,2048]{2,1,0:T(2,128)(2,1)S(1)}, bf16[1,1,2048]{2,1,0:T(2,128)(2,1)}, u32[]{:S(2)}) copy-start(bf16[1,1,2048]{2,1,0:T(2,128)(2,1)} %param.18) | copy-start | bytes 12292
  1201.8 1875.3 %all-gather.11.cloned.1.call-start = ((), (), s32[]{:S(2)}) async-start(), calls=%async_computation.5 | async-start | bytes 4202496 | tf_op jit(solution)/shard_map/all_gather | solution.py:186
  1688.6 2830.8 %all-gather.9.cloned.1.call-start = ((), (), s32[]{:S(2)}) async-start(), calls=%async_computation.4 | async-start | bytes 16809984 | tf_op jit(solution)/shard_map/all_gather | solution.py:199
  3077.2 4.8 copy-start.4
  4534.7 1.6 copy-start.9
  4534.7 1.6 copy-start.10
  4534.7 7.1 copy-start.1
Sparse Core Ops, SparseCore 0:
  116.6 1056.8 all-gather.6
  1202.0 481.1 all-reduce.2
  1688.8 1388.3 all-gather.10
  3082.7 1436.6 all-gather.8
